TPU v7x, 512 devices: a whole 4x8x8 slice. The times are simulated.
512 devices in a mesh: grp: 16 (over y, core), dom: 32 (over x, z).
Axes of the slice: x: 4, y: 8, z: 8, core: 2. Of those that a mesh axis runs over, the one named last changes fastest.
Arguments:
- owned_blips: bfloat16 [2048, 32768], P(('grp', 'dom')), may hold values from -6 to 6
- potential: float32 [32, 512, 1024], P('dom', 'grp'), may hold values from -5 to 5
- slot_owner: int32 [12288, 1], P(('grp', 'dom')), may hold values from 0 to 31; in each aligned block of 24 rows (0 to 23, 24 to 47, ...) at most 2 rows name the same one
- slot_row: int32 [12288], P(('grp', 'dom')), may hold values from 0 to 3
- slot_offset: int32 [12288], P(('grp', 'dom')), may hold values from 0 to 31
Outputs:
- blip_gradient: float32 [2048, 32768], P(('grp', 'dom'))
- hamiltonian: float32 [2048, 128], P(('grp', 'dom'))
Inputs may be any that keep to these rules, and one draw needn't show every extreme that they name: `slot_owner`: among the 24 pieces of one device at most 2 name the same owner.
All inputs are finite; a program needn't handle non-finite values.
Results may differ from a plain program's by a relative error of at most 0.012.
The roundings to bfloat16 on the way count: a program that leaves them out, or rounds other values in their place, can miss the bound.
Values may be sent and summed in bfloat16 or wider, within the bound.
No kernel may reach another device: no remote copies, remote signals or barrier semaphores. Data moves between devices by JAX's collectives and lax.ppermute only.
A program may use at most 128 MiB of HBM per device.

v0:
```python
import jax
import jax.numpy as jnp
from jax import lax
from jax.sharding import PartitionSpec as P

NB = 32


def passed_along(block, axis, distance):
    devices = range(lax.axis_size(axis))
    route = [((i - distance) % len(devices), i) for i in devices]
    return lax.ppermute(block, axis, route)


def spline_tables():
    cells_line = jnp.arange(NB, dtype=jnp.int32)
    offset = cells_line[:, None] - cells_line[None, :]
    spline = jnp.where(
        offset == 0, 2.0 / 3.0, jnp.where(jnp.abs(offset) == 1, 1.0 / 6.0, 0.0)
    ).astype(jnp.float32)
    second = jnp.where(offset == 0, -2.0, jnp.where(jnp.abs(offset) == 1, 1.0, 0.0)).astype(
        jnp.float32
    )
    plane_value = jnp.einsum("ac,bd->abcd", spline, spline).reshape(NB * NB, NB * NB)
    plane_curve = (
        jnp.einsum("ac,bd->abcd", second, spline) + jnp.einsum("ac,bd->abcd", spline, second)
    ).reshape(NB * NB, NB * NB)
    return (
        spline.astype(jnp.bfloat16),
        second.astype(jnp.bfloat16),
        plane_value.astype(jnp.bfloat16),
        plane_curve.astype(jnp.bfloat16),
    )


def on_device(owned_blips, potential, slot_owner, slot_row, slot_offset):
    spline, second, plane_value, plane_curve = spline_tables()
    domain_count = lax.axis_size("dom")
    slot_count = slot_row.shape[0]
    owned_count = owned_blips.shape[0]
    cell_count = owned_blips.shape[1]
    plane_cells = NB * NB
    capacity = max(2, -(-slot_count // domain_count))
    group_size = domain_count * owned_count
    owner_of = slot_owner[:, 0]
    target = owner_of * owned_count + slot_row
    owner_hot = (owner_of[:, None] == jnp.arange(domain_count, dtype=jnp.int32)[None, :]).astype(
        jnp.int32
    )
    position = jnp.sum(jnp.cumsum(owner_hot, axis=0) * owner_hot, axis=1) - 1
    place_slot = owner_of * capacity + position
    place_hot = place_slot[None, :] == jnp.arange(domain_count * capacity, dtype=jnp.int32)[:, None]
    asked_rows = jnp.sum(jnp.where(place_hot, slot_row[None, :], 0), axis=1) + owned_count * (
        1 - jnp.sum(place_hot.astype(jnp.int32), axis=1)
    )
    place_low = place_hot.astype(jnp.bfloat16)
    gathered_rows = lax.all_gather(owned_blips, "dom", axis=0, tiled=True)
    chosen = (
        target[:, None] == jnp.arange(gathered_rows.shape[0], dtype=jnp.int32)[None, :]
    ).astype(jnp.bfloat16)
    slot_blips = jnp.dot(chosen, gathered_rows, preferred_element_type=jnp.float32).astype(
        jnp.bfloat16
    )
    upper_cells = passed_along(potential, "grp", -1)
    extended = jnp.concatenate([potential[0], upper_cells[0]], axis=0)

    def cut_window(first_row):
        return lax.dynamic_slice_in_dim(extended, first_row, NB, 0)

    window = jax.vmap(cut_window)(slot_offset)
    layered = slot_blips.reshape(slot_count, NB, plane_cells)
    y_value = jnp.einsum("ya,sab->syb", spline, layered, preferred_element_type=jnp.float32).astype(
        jnp.bfloat16
    )
    y_curve = jnp.einsum("ya,sab->syb", second, layered, preferred_element_type=jnp.float32).astype(
        jnp.bfloat16
    )
    flat_value = y_value.reshape(-1, plane_cells)
    values_grid = jnp.dot(flat_value, plane_value, preferred_element_type=jnp.float32)
    laplace = jnp.dot(
        y_curve.reshape(-1, plane_cells), plane_value, preferred_element_type=jnp.float32
    ) + jnp.dot(flat_value, plane_curve, preferred_element_type=jnp.float32)
    applied = (-0.5 * laplace + window.reshape(-1, plane_cells) * values_grid).astype(jnp.bfloat16)
    values_low = values_grid.astype(jnp.bfloat16)
    back_plane = jnp.dot(applied, plane_value, preferred_element_type=jnp.float32).astype(
        jnp.bfloat16
    )
    gradient_piece = jnp.einsum(
        "ay,sab->syb",
        spline,
        back_plane.reshape(slot_count, NB, plane_cells),
        preferred_element_type=jnp.float32,
    ).astype(jnp.bfloat16)
    intersection = lax.dot_general(
        values_low.reshape(slot_count, cell_count),
        applied.reshape(slot_count, cell_count),
        (((1,), (1,)), ((), ())),
        preferred_element_type=jnp.float32,
    ) / float(cell_count)
    select_full = (target[:, None] == jnp.arange(group_size, dtype=jnp.int32)[None, :]).astype(
        jnp.float32
    )
    weighted = jnp.dot(intersection, select_full, precision=lax.Precision.HIGHEST)
    place_f32 = place_hot.astype(jnp.float32)
    send_ham = jnp.concatenate(
        [
            jnp.dot(place_f32, weighted, precision=lax.Precision.HIGHEST),
            asked_rows.astype(jnp.float32)[:, None],
        ],
        axis=1,
    ).reshape(domain_count, capacity, group_size + 1)
    got_ham = lax.all_to_all(send_ham, "dom", split_axis=0, concat_axis=0, tiled=True).reshape(
        domain_count * capacity, group_size + 1
    )
    got_rows = got_ham[:, group_size]
    send_grad = jnp.dot(
        place_low,
        gradient_piece.reshape(slot_count, cell_count),
        preferred_element_type=jnp.bfloat16,
    ).reshape(domain_count, capacity, cell_count)
    got_grad = lax.all_to_all(send_grad, "dom", split_axis=0, concat_axis=0, tiled=True)
    row_hot = got_rows[None, :] == jnp.arange(owned_count, dtype=jnp.float32)[:, None]
    hamilton = jnp.dot(
        row_hot.astype(jnp.float32), got_ham[:, :group_size], precision=lax.Precision.HIGHEST
    )
    gradient = jnp.dot(
        row_hot.astype(jnp.bfloat16),
        got_grad.reshape(-1, cell_count),
        preferred_element_type=jnp.float32,
    )
    return (gradient, hamilton)


def solution(mesh):
    placed = (
        P(("grp", "dom"), None),
        P("dom", "grp", None),
        P(("grp", "dom"), None),
        P(("grp", "dom")),
        P(("grp", "dom")),
    )
    return jax.shard_map(
        on_device,
        mesh=mesh,
        in_specs=placed,
        out_specs=(P(("grp", "dom"), None), P(("grp", "dom"), None)),
        check_vma=False,
    )
```

profile of v0, /device:TPU:8, one launch (start us, length us, event | category | flops | bytes accessed | tf_op | source)
XLA Modules:
  0.0 299.2 jit_solution(602557687519509434)
XLA Ops:
  11.2 7.6 %fusion.1 = (bf16[32,32,32,32]{3,2,1,0:T(8,128)(2,1)}, bf16[32,32,32,32]{3,2,1,0:T(8,128)(2,1)}) fusion(f32[32,32]{1,0:T(8,128)S(1)} %copy.43, f32[32,32]{1,0:T(8,128)S(1)} %copy.40), kind=kLoop, calls=%fused_computation.6 | loop fusion | flops 6291456 | bytes 4202496 | tf_op jit(solution)/shard_map/convert_element_type | solution.py:32
  18.7 12.4 %convert_element_type.92 = bf16[1024,1024]{1,0:T(8,128)(2,1)} reshape(bf16[32,32,32,32]{3,2,1,0:T(8,128)(2,1)} %get-tuple-element.21) | data formatting | bytes 4194304 | tf_op jit(solution)/shard_map/convert_element_type | solution.py:31
  31.1 11.4 %convert_element_type.99 = bf16[1024,1024]{1,0:T(8,128)(2,1)S(1)} reshape(bf16[32,32,32,32]{3,2,1,0:T(8,128)(2,1)} %get-tuple-element.20) | data formatting | bytes 4194304 | tf_op jit(solution)/shard_map/convert_element_type | solution.py:32
  42.8 45.6 %while.1 = (s32[]{:T(128)}, f32[64,1024]{1,0:T(8,128)S(1)}, s32[24,2]{0,1:T(2,128)S(1)}, f32[24,32,1024]{2,1,0:T(8,128)}, s32[]{:T(128)}) while((s32[]{:T(128)}, f32[64,1024]{1,0:T(8,128)S(1)}, s32[24,2]{0,1:T(2,128)S(1)}, f32[24,32,1024]{2,1,0:T(8,128)}, s32[]{:T(128)}) %tuple.24), condition=%wide.while_cond, body=%wide.while_body.sunk | while | flops 2 | bytes 263257 | solution.py:68
  52.9 1.3 bitcast_dynamic-update-slice_fusion.2
  54.8 1.3 bitcast_dynamic-update-slice_fusion.2
  58.5 1.3 bitcast_dynamic-update-slice_fusion.2
  64.2 1.3 bitcast_dynamic-update-slice_fusion.2
  66.1 1.3 bitcast_dynamic-update-slice_fusion.2
  69.9 1.3 bitcast_dynamic-update-slice_fusion.2
  75.6 1.3 bitcast_dynamic-update-slice_fusion.2
  77.5 1.3 bitcast_dynamic-update-slice_fusion.2
  81.3 1.3 bitcast_dynamic-update-slice_fusion.2
  85.1 1.3 bitcast_dynamic-update-slice_fusion.2
  87.0 1.3 bitcast_dynamic-update-slice_fusion.2
  88.4 31.4 %all-gather.3.cloned.1.call-done = bf16[32,4,32768]{2,1,0:T(4,128)(2,1)} async-done(((bf16[1,4,32768]{2,1,0:T(4,128)(2,1)}), bf16[32,4,32768]{2,1,0:T(4,128)(2,1)}) %all-gather.3.cloned.1.call-update) | async-done | bytes 8388624 | tf_op jit(solution)/shard_map/all_gather | solution.py:57
  119.8 12.7 %reshape.138 = bf16[128,32768]{1,0:T(8,128)(2,1)} reshape(bf16[32,4,32768]{2,1,0:T(4,128)(2,1)} %all-gather.3.cloned.1.call-done) | data formatting | bytes 16777216
  132.4 4.6 %convolution_convert_fusion = bf16[24,32768]{1,0:T(8,128)(2,1)S(1)} fusion(bf16[128,32768]{1,0:T(8,128)(2,1)} %reshape.138, s32[24]{0:T(128)S(1)} %get-tuple-element.23), kind=kOutput, calls=%fused_computation.2 | convolution fusion | flops 202116096 | bytes 9961568 | tf_op jit(solution)/shard_map/dot_general | solution.py:61
  140.2 3.0 fusion.44
  143.2 1.8 fusion.45
  145.1 3.1 %fusion.3 = bf16[768,1024]{1,0:T(8,128)(2,1)} fusion(f32[768,1024]{1,0:T(8,128)S(1)} %get-tuple-element.25, f32[24,32,1024]{2,1,0:T(8,128)S(1)} %copy-done.1, f32[768,1024]{1,0:T(8,128)S(1)} %fusion.45, bf16[768,1024]{1,0:T(8,128)(2,1)S(1)} %bitcast.71, bf16[1024,1024]{1,0:T(8,128)(2,1)S(1)} %convert_element_type.99), kind=kOutput, calls=%fused_computation.9 | convolution fusion | flops 1614544896 | bytes 14680064 | tf_op jit(solution)/shard_map/dot_general | solution.py:82
  148.1 2.7 reshape.113
  150.8 4.5 %convolution_convert_fusion.4 = bf16[768,1024]{1,0:T(8,128)(2,1)} fusion(bf16[768,1024]{1,0:T(8,128)(2,1)S(1)} %copy-done, bf16[1024,1024]{1,0:T(8,128)(2,1)} %convert_element_type.92), kind=kOutput, calls=%fused_computation.13 | convolution fusion | flops 1611399168 | bytes 5242880 | tf_op jit(solution)/shard_map/dot_general | solution.py:85
  155.4 2.6 reshape.110
  159.7 5.7 %all-to-all-start = ((f32[32,2,129]{2,1,0:T(2,128)}), f32[32,2,129]{2,1,0:T(2,128)S(1)}, u32[]{:S(2)}, u32[]{:S(2)}) async-start(f32[32,2,129]{2,1,0:T(2,128)} %pad_maximum_fusion.1), calls=%async_computation | async-start | bytes 131072 | tf_op jit(solution)/shard_map/all_to_all | solution.py:112
  165.4 2.0 fusion.4
  168.2 1.4 fusion.7
  169.5 6.3 %copy.46 = bf16[32,2,32768]{2,1,0:T(2,128)(2,1)} copy(bf16[32,2,32768]{2,0,1:T(8,128)(2,1)S(1)} %fusion.7) | data formatting | bytes 8388608 | tf_op jit(solution)/shard_map/dot_general | solution.py:116
  175.8 9.7 %all-to-all-start.1 = ((bf16[32,2,32768]{2,1,0:T(2,128)(2,1)}), bf16[32,2,32768]{2,1,0:T(2,128)(2,1)}, u32[]{:S(2)}, u32[]{:S(2)}) async-start(bf16[32,2,32768]{2,1,0:T(2,128)(2,1)} %copy.46), calls=%async_computation.1 | async-start | bytes 8388608 | tf_op jit(solution)/shard_map/all_to_all | solution.py:121
  186.4 95.0 %all-to-all-done.1 = bf16[32,2,32768]{2,1,0:T(2,128)(2,1)} async-done(((bf16[32,2,32768]{2,1,0:T(2,128)(2,1)}), bf16[32,2,32768]{2,1,0:T(2,128)(2,1)}, u32[]{:S(2)}, u32[]{:S(2)}) %all-to-all-start.1) | async-done | bytes 4194336 | tf_op jit(solution)/shard_map/all_to_all | solution.py:121
  281.4 7.3 %reshape.117 = bf16[64,32768]{1,0:T(8,128)(2,1)} reshape(bf16[32,2,32768]{2,1,0:T(2,128)(2,1)} %all-to-all-done.1) | data formatting | bytes 8388608 | tf_op jit(solution)/shard_map/reshape | solution.py:128
  288.7 3.6 %fusion.25 = f32[4,32768]{1,0:T(4,128)} fusion(bf16[64,32768]{1,0:T(8,128)(2,1)} %reshape.117, f32[64]{0:T(128)S(1)} %slice_reduce_fusion), kind=kOutput, calls=%fused_computation.49 | convolution fusion | flops 16777472 | bytes 4718848 | tf_op jit(solution)/shard_map/dot_general | solution.py:126
  (103 shorter events, 41.8 us)
Async XLA Ops:
  7.2 112.6 %all-gather.3.cloned.1.call-start = ((), (), s32[]{:S(2)}) async-start(), calls=%async_computation.2 | async-start | bytes 8650752 | tf_op jit(solution)/shard_map/all_gather | solution.py:57
  7.9 34.8 %collective-permute-start = (f32[1,32,1024]{2,1,0:T(8,128)}, f32[1,32,1024]{2,1,0:T(8,128)S(1)}, u32[]{:S(2)}, u32[]{:S(2)}) collective-permute-start(f32[1,32,1024]{2,1,0:T(8,128)} %param.6), channel_id=1, source_target_pairs={{32,0},{64,32},{96,64},{128,96},{160,128},{192,160},{224,192},{256... | collective-permute-start | bytes 393224 | tf_op jit(solution)/shard_map/ppermute | solution.py:12
  11.1 7.6 %copy-start.4 = (s32[24]{0:T(128)S(1)}, s32[24]{0:T(128)}, u32[]{:S(2)}) copy-start(s32[24]{0:T(128)} %param.9) | copy-start | bytes 292
  31.1 11.6 %copy-start.3 = (f32[1,32,1024]{2,1,0:T(8,128)S(1)}, f32[1,32,1024]{2,1,0:T(8,128)}, u32[]{:S(2)}) copy-start(f32[1,32,1024]{2,1,0:T(8,128)} %param.6) | copy-start | bytes 393220
  138.6 1.6 copy-start.2
  143.2 1.9 copy-start.1
  148.1 2.7 copy-start
  159.7 16.1 %all-to-all-start = ((f32[32,2,129]{2,1,0:T(2,128)}), f32[32,2,129]{2,1,0:T(2,128)S(1)}, u32[]{:S(2)}, u32[]{:S(2)}) async-start(f32[32,2,129]{2,1,0:T(2,128)} %pad_maximum_fusion.1), calls=%async_computation | async-start | bytes 131072 | tf_op jit(solution)/shard_map/all_to_all | solution.py:112
  175.8 105.6 %all-to-all-start.1 = ((bf16[32,2,32768]{2,1,0:T(2,128)(2,1)}), bf16[32,2,32768]{2,1,0:T(2,128)(2,1)}, u32[]{:S(2)}, u32[]{:S(2)}) async-start(bf16[32,2,32768]{2,1,0:T(2,128)(2,1)} %copy.46), calls=%async_computation.1 | async-start | bytes 8388608 | tf_op jit(solution)/shard_map/all_to_all | solution.py:121
Sparse Core Ops, SparseCore 0:
  11.1 108.5 all-gather.2
where the time goes:
time: 301 us; the launch traced here: 299 us
  waiting for transfers between devices  127 us (42%)
  local copies, waits for them, and re-layouts  104 us (35%)
  matrix products  27.1 us (9%)
  starting transfers between devices  15.4 us (5%)
  between operations  14.3 us (5%)
  other arithmetic  11.3 us (4%)
    all_to_all x1, waiting for transfers between devices, on_device(): lax.all_to_all(send_grad, 'dom', split_axis=0, concat_axis=0, tiled=True)  95 us
    gather x72, local copies, waits for them, and re-layouts  45.5 us
    all_gather x1, waiting for transfers between devices, on_device(): gathered_rows = lax.all_gather(owned_blips, 'dom', axis=0, tiled=True)  31.4 us
    unnamed x12, local copies, waits for them, and re-layouts  14.5 us
    convert_element_type x1, local copies, waits for them, and re-layouts, spline_tables(): plane_value.astype(jnp.bfloat16)  12.4 us
    convert_element_type x1, local copies, waits for them, and re-layouts, spline_tables(): plane_curve.astype(jnp.bfloat16)  11.4 us
    all_to_all x1, starting transfers between devices, on_device(): lax.all_to_all(send_grad, 'dom', split_axis=0, concat_axis=0, tiled=True)  9.69 us
    convert_element_type x1, other arithmetic, spline_tables(): plane_curve.astype(jnp.bfloat16)  7.56 us
  transfers between devices with their start and end apart: 4, of which 2 were waited for; matrix products, arithmetic and copies ran while one was open for 31% of the time, Pallas kernels for 0%

commit v1 on v0

--- a/solution.py
+++ b/solution.py
@@ -54,7 +54,9 @@
         1 - jnp.sum(place_hot.astype(jnp.int32), axis=1)
     )
     place_low = place_hot.astype(jnp.bfloat16)
-    gathered_rows = lax.all_gather(owned_blips, "dom", axis=0, tiled=True)
+    gathered_rows = jnp.concatenate(
+        lax.all_to_all(jnp.stack([owned_blips] * lax.axis_size("dom")), "dom", 0, 0), axis=0
+    )
     chosen = (
         target[:, None] == jnp.arange(gathered_rows.shape[0], dtype=jnp.int32)[None, :]
     ).astype(jnp.bfloat16)

time: 301 us -> 390 us (1.30)
  the two profiles are of different devices: /device:TPU:8 before, /device:TPU:1 now
where the time goes in v1:
time: 390 us; the launch traced here: 389 us
  waiting for transfers between devices  205 us (53%)
  local copies, waits for them, and re-layouts  112 us (29%)
  starting transfers between devices  34.8 us (9%)
  matrix products  27.1 us (7%)
  other arithmetic  8.69 us (2%)
    all_to_all x1, waiting for transfers between devices, on_device(): lax.all_to_all(jnp.stack([owned_blips] * lax.axis_size('dom')), 'dom', 0, 0)  109 us
    all_to_all x1, waiting for transfers between devices, on_device(): lax.all_to_all(send_grad, 'dom', split_axis=0, concat_axis=0, tiled=True)  95.8 us
    gather x72, local copies, waits for them, and re-layouts  45.6 us
    all_to_all x1, starting transfers between devices, on_device(): lax.all_to_all(jnp.stack([owned_blips] * lax.axis_size('dom')), 'dom', 0, 0)  14 us
    reshape x1, local copies, waits for them, and re-layouts, on_device(): jnp.concatenate(lax.all_to_all(jnp.stack([owned_blips] * lax.axis_size('d...  12.7 us
    convert_element_type x1, local copies, waits for them, and re-layouts, spline_tables(): plane_value.astype(jnp.bfloat16)  12.4 us
    convert_element_type x1, local copies, waits for them, and re-layouts, spline_tables(): plane_curve.astype(jnp.bfloat16)  11.3 us
    all_to_all x1, starting transfers between devices, on_device(): lax.all_to_all(send_ham, 'dom', split_axis=0, concat_axis=0, tiled=True)  10.8 us
  transfers between devices with their start and end apart: 4, of which 2 were waited for; matrix products, arithmetic and copies ran while one was open for 23% of the time, Pallas kernels for 0%

profile of v1, /device:TPU:1, one launch (start us, length us, event | category | flops | bytes accessed | tf_op | source)
XLA Modules:
  0.0 388.6 jit_solution(1533134316209974466)
XLA Ops:
  0.6 7.9 %stack.2 = bf16[32,4,32768]{2,1,0:T(4,128)(2,1)} broadcast(bf16[4,32768]{1,0:T(4,128)(2,1)} %param.5), dimensions={1,2} | broadcast | bytes 8650752 | tf_op jit(solution)/shard_map/stack | solution.py:58
  8.6 14.0 %all-to-all-start = ((bf16[32,4,32768]{2,1,0:T(4,128)(2,1)}), bf16[32,4,32768]{2,1,0:T(4,128)(2,1)}, u32[]{:S(2)}, u32[]{:S(2)}) async-start(bf16[32,4,32768]{2,1,0:T(4,128)(2,1)} %stack.2), calls=%async_computation | async-start | bytes 16777216 | tf_op jit(solution)/shard_map/all_to_all | solution.py:58
  24.1 7.6 %fusion.1 = (bf16[32,32,32,32]{3,2,1,0:T(8,128)(2,1)}, bf16[32,32,32,32]{3,2,1,0:T(8,128)(2,1)}) fusion(f32[32,32]{1,0:T(8,128)S(1)} %copy.43, f32[32,32]{1,0:T(8,128)S(1)} %copy.40), kind=kLoop, calls=%fused_computation.6 | loop fusion | flops 6291456 | bytes 4202496 | tf_op jit(solution)/shard_map/convert_element_type | solution.py:32
  31.7 12.4 %convert_element_type.92 = bf16[1024,1024]{1,0:T(8,128)(2,1)} reshape(bf16[32,32,32,32]{3,2,1,0:T(8,128)(2,1)} %get-tuple-element.21) | data formatting | bytes 4194304 | tf_op jit(solution)/shard_map/convert_element_type | solution.py:31
  44.1 11.3 %convert_element_type.99 = bf16[1024,1024]{1,0:T(8,128)(2,1)S(1)} reshape(bf16[32,32,32,32]{3,2,1,0:T(8,128)(2,1)} %get-tuple-element.20) | data formatting | bytes 4194304 | tf_op jit(solution)/shard_map/convert_element_type | solution.py:32
  55.7 45.7 %while.1 = (s32[]{:T(128)}, f32[64,1024]{1,0:T(8,128)S(1)}, s32[24,2]{0,1:T(2,128)S(1)}, f32[24,32,1024]{2,1,0:T(8,128)}, s32[]{:T(128)}) while((s32[]{:T(128)}, f32[64,1024]{1,0:T(8,128)S(1)}, s32[24,2]{0,1:T(2,128)S(1)}, f32[24,32,1024]{2,1,0:T(8,128)}, s32[]{:T(128)}) %tuple.24), condition=%wide.while_cond, body=%wide.while_body.sunk | while | flops 2 | bytes 263257 | solution.py:70
  62.0 1.3 bitcast_dynamic-update-slice_fusion.2
  65.8 1.3 bitcast_dynamic-update-slice_fusion.2
  73.4 1.3 bitcast_dynamic-update-slice_fusion.2
  81.0 1.3 bitcast_dynamic-update-slice_fusion.2
  82.9 1.3 bitcast_dynamic-update-slice_fusion.2
  86.7 1.3 bitcast_dynamic-update-slice_fusion.2
  90.5 1.3 bitcast_dynamic-update-slice_fusion.2
  94.3 1.3 bitcast_dynamic-update-slice_fusion.2
  100.0 1.3 bitcast_dynamic-update-slice_fusion.2
  101.3 109.4 %all-to-all-done = bf16[32,4,32768]{2,1,0:T(4,128)(2,1)} async-done(((bf16[32,4,32768]{2,1,0:T(4,128)(2,1)}), bf16[32,4,32768]{2,1,0:T(4,128)(2,1)}, u32[]{:S(2)}, u32[]{:S(2)}) %all-to-all-start) | async-done | bytes 8388640 | tf_op jit(solution)/shard_map/all_to_all | solution.py:58
  210.7 12.7 %reshape.113 = bf16[128,32768]{1,0:T(8,128)(2,1)} reshape(bf16[32,4,32768]{2,1,0:T(4,128)(2,1)} %all-to-all-done) | data formatting | bytes 16777216 | tf_op jit(solution)/shard_map/reshape | solution.py:57
  223.4 4.6 %convolution_convert_fusion = bf16[24,32768]{1,0:T(8,128)(2,1)S(1)} fusion(bf16[128,32768]{1,0:T(8,128)(2,1)} %reshape.113, s32[24]{0:T(128)S(1)} %get-tuple-element.23), kind=kOutput, calls=%fused_computation.2 | convolution fusion | flops 202116096 | bytes 9961568 | tf_op jit(solution)/shard_map/dot_general | solution.py:63
  231.2 3.0 fusion.44
  234.1 1.8 fusion.45
  236.0 3.0 fusion.3
  239.1 2.7 reshape.119
  241.8 4.5 %convolution_convert_fusion.4 = bf16[768,1024]{1,0:T(8,128)(2,1)} fusion(bf16[768,1024]{1,0:T(8,128)(2,1)S(1)} %copy-done, bf16[1024,1024]{1,0:T(8,128)(2,1)} %convert_element_type.92), kind=kOutput, calls=%fused_computation.13 | convolution fusion | flops 1611399168 | bytes 5242880 | tf_op jit(solution)/shard_map/dot_general | solution.py:87
  246.3 2.6 reshape.116
  250.7 10.8 %all-to-all-start.1 = ((f32[32,2,129]{2,1,0:T(2,128)}), f32[32,2,129]{2,1,0:T(2,128)S(1)}, u32[]{:S(2)}, u32[]{:S(2)}) async-start(f32[32,2,129]{2,1,0:T(2,128)} %pad_maximum_fusion.1), calls=%async_computation.1 | async-start | bytes 131072 | tf_op jit(solution)/shard_map/all_to_all | solution.py:114
  261.5 2.0 fusion.4
  264.2 1.4 fusion.7
  265.6 6.3 %copy.46 = bf16[32,2,32768]{2,1,0:T(2,128)(2,1)} copy(bf16[32,2,32768]{2,0,1:T(8,128)(2,1)S(1)} %fusion.7) | data formatting | bytes 8388608 | tf_op jit(solution)/shard_map/dot_general | solution.py:118
  271.9 9.1 %all-to-all-start.2 = ((bf16[32,2,32768]{2,1,0:T(2,128)(2,1)}), bf16[32,2,32768]{2,1,0:T(2,128)(2,1)}, u32[]{:S(2)}, u32[]{:S(2)}) async-start(bf16[32,2,32768]{2,1,0:T(2,128)(2,1)} %copy.46), calls=%async_computation.2 | async-start | bytes 8388608 | tf_op jit(solution)/shard_map/all_to_all | solution.py:123
  281.9 95.8 %all-to-all-done.2 = bf16[32,2,32768]{2,1,0:T(2,128)(2,1)} async-done(((bf16[32,2,32768]{2,1,0:T(2,128)(2,1)}), bf16[32,2,32768]{2,1,0:T(2,128)(2,1)}, u32[]{:S(2)}, u32[]{:S(2)}) %all-to-all-start.2) | async-done | bytes 4194336 | tf_op jit(solution)/shard_map/all_to_all | solution.py:123
  377.7 7.3 %reshape.123 = bf16[64,32768]{1,0:T(8,128)(2,1)} reshape(bf16[32,2,32768]{2,1,0:T(2,128)(2,1)} %all-to-all-done.2) | data formatting | bytes 8388608 | tf_op jit(solution)/shard_map/reshape | solution.py:130
  385.0 3.6 fusion.25
  (107 shorter events, 42.1 us)
Async XLA Ops:
  8.6 14.0 %copy-start.3 = (f32[1,32,1024]{2,1,0:T(8,128)S(1)}, f32[1,32,1024]{2,1,0:T(8,128)}, u32[]{:S(2)}) copy-start(f32[1,32,1024]{2,1,0:T(8,128)} %param.6) | copy-start | bytes 393220
  8.6 15.1 %copy-start.4 = (s32[24,1]{0,1:T(1,128)S(1)}, s32[24,1]{0,1:T(1,128)}, u32[]{:S(2)}) copy-start(s32[24,1]{0,1:T(1,128)} %param.7) | copy-start | bytes 292
  8.6 15.4 %copy-start.5 = (s32[24]{0:T(128)S(1)}, s32[24]{0:T(128)}, u32[]{:S(2)}) copy-start(s32[24]{0:T(128)} %param.8) | copy-start | bytes 292
  8.6 202.2 %all-to-all-start = ((bf16[32,4,32768]{2,1,0:T(4,128)(2,1)}), bf16[32,4,32768]{2,1,0:T(4,128)(2,1)}, u32[]{:S(2)}, u32[]{:S(2)}) async-start(bf16[32,4,32768]{2,1,0:T(4,128)(2,1)} %stack.2), calls=%async_computation | async-start | bytes 16777216 | tf_op jit(solution)/shard_map/all_to_all | solution.py:58
  22.6 33.1 %collective-permute-start = (f32[1,32,1024]{2,1,0:T(8,128)S(1)}, f32[1,32,1024]{2,1,0:T(8,128)S(1)}, u32[]{:S(2)}, u32[]{:S(2)}) collective-permute-start(f32[1,32,1024]{2,1,0:T(8,128)S(1)} %copy-done.3), channel_id=1, source_target_pairs={{32,0},{64,32},{96,64},{128,96},{160,128},{192,160},{224,192},{256... | collective-permute-start | bytes 393224 | tf_op jit(solution)/shard_map/ppermute | solution.py:12
  24.1 7.6 %copy-start.6 = (s32[24]{0:T(128)S(1)}, s32[24]{0:T(128)}, u32[]{:S(2)}) copy-start(s32[24]{0:T(128)} %param.9) | copy-start | bytes 292
  229.6 1.6 copy-start.2
  234.1 1.9 copy-start.1
  239.1 2.7 copy-start
  250.7 21.2 %all-to-all-start.1 = ((f32[32,2,129]{2,1,0:T(2,128)}), f32[32,2,129]{2,1,0:T(2,128)S(1)}, u32[]{:S(2)}, u32[]{:S(2)}) async-start(f32[32,2,129]{2,1,0:T(2,128)} %pad_maximum_fusion.1), calls=%async_computation.1 | async-start | bytes 131072 | tf_op jit(solution)/shard_map/all_to_all | solution.py:114
  271.9 105.8 %all-to-all-start.2 = ((bf16[32,2,32768]{2,1,0:T(2,128)(2,1)}), bf16[32,2,32768]{2,1,0:T(2,128)(2,1)}, u32[]{:S(2)}, u32[]{:S(2)}) async-start(bf16[32,2,32768]{2,1,0:T(2,128)(2,1)} %copy.46), calls=%async_computation.2 | async-start | bytes 8388608 | tf_op jit(solution)/shard_map/all_to_all | solution.py:123
